TPU v7x, 128 devices: a whole 4x4x4 slice. The times are simulated.
128 devices in a mesh: seq: 32 (over y, x, core), head: 4 (over z).
Axes of the slice: x: 4, y: 4, z: 4, core: 2. Of those that a mesh axis runs over, the one named last changes fastest.
Arguments:
- value_rows: bfloat16 [8192, 4096], P('seq', 'head'), may hold values from -6 to 6
- key_rows: bfloat16 [8192, 4096], P('seq', 'head'), may hold values from -6 to 6
- query_rows: bfloat16 [8192, 4096], P('seq', 'head'), may hold values from -6 to 6
- cotangent: bfloat16 [8192, 4096], P('seq', 'head'), may hold values from -6 to 6
- filter_taps: float32 [16, 2048], replicated, may hold values from -0.125 to 0.125
- doc_blocks: int32 [64], replicated, may hold values from 0 to 15, never falling along the last dimension, each value on 1 to 12 neighbouring positions
Outputs:
- output_rows: bfloat16 [8192, 4096], P('seq', 'head')
- grad_query: bfloat16 [8192, 4096], P('seq', 'head')
- grad_key: bfloat16 [8192, 4096], P('seq', 'head')
- grad_value: bfloat16 [8192, 4096], P('seq', 'head')
- grad_filter: float32 [16, 2048], replicated
Inputs may be any that keep to these rules, and one draw needn't show every extreme that they name: doc_blocks gives each 128-token block its document number; numbers never fall, each document spans 1 to 12 blocks, and one spans exactly 12.
All inputs are finite; a program needn't handle non-finite values.
Results may differ from a plain program's by a relative error of at most 0.0058.
Values may be sent and summed in bfloat16 or wider, within the bound.
No kernel may reach another device: no remote copies, remote signals or barrier semaphores. Data moves between devices by JAX's collectives and lax.ppermute only.
A program may use at most 384 MiB of HBM per device.

v0:
```python
import numpy as np
import jax
import jax.numpy as jnp
from jax import lax
from jax.experimental import pallas as pl
from jax.experimental.pallas import tpu as pltpu
from jax.sharding import PartitionSpec as P

DH = 64
BLK = 128


def passed_along(value, axis, by):
    length = lax.axis_size(axis)
    pairs = [(i, i + by) for i in range(length) if 0 <= i + by < length]
    return lax.ppermute(value, axis, pairs)


def tap_rows(rounded, index):
    filters, taps_total = rounded.shape
    padded = jnp.concatenate([rounded, jnp.zeros((filters, 1), jnp.float32)], 1)
    safe = np.where((index >= 0) & (index < taps_total), index, taps_total)
    return jnp.take(padded, jnp.asarray(safe, jnp.int32), axis=1)


def make_kernel(nb, lags, width, span, conv_start):
    def kernel(qc_ref, qa_ref, cm_ref, pext_ref, sext_ref, srev_ref, q_ref, ct_ref,
               k_ref, v_ref, out_ref, gq_ref, gk_ref, gv_ref, gd_ref):
        step = pl.program_id(0)
        lo = lax.broadcasted_iota(jnp.int32, (BLK, BLK), 1) < DH

        def table(ref, i, shift):
            row = ref[pl.ds(2 * step + i, 1), :]
            full = jnp.broadcast_to(row, (BLK, span))
            rolled = pltpu.roll(full, shift, 1, stride=1, stride_axis=0)
            return rolled[:, :width]

        tc = jnp.concatenate(
            [table(qc_ref, 0, span - (BLK - 1)), table(qc_ref, 1, span - (BLK - 1))], 0
        )
        ta = jnp.concatenate([table(qa_ref, 0, span - BLK), table(qa_ref, 1, span - BLK)], 0)
        gsum = jnp.zeros((2 * BLK, width), jnp.float32)
        for n in range(nb):
            rows = pl.ds(n * BLK, BLK)
            cmask = cm_ref[n : n + 1, :]
            amask = cm_ref[nb + n : nb + n + 1, :]
            pw = pext_ref[pl.ds(conv_start + n * BLK, width), :]
            sw = sext_ref[pl.ds(n * BLK, width), :]
            conv2 = jnp.dot(
                (tc * cmask).astype(jnp.bfloat16), pw, preferred_element_type=jnp.float32
            )
            conv = jnp.where(lo, conv2[:BLK], conv2[BLK:])
            adj2 = jnp.dot(
                (ta * amask).astype(jnp.bfloat16), sw, preferred_element_type=jnp.float32
            )
            adj = jnp.where(lo, adj2[:BLK], adj2[BLK:])
            out_ref[rows, :] = (q_ref[rows, :].astype(jnp.float32) * conv).astype(jnp.bfloat16)
            gq_ref[rows, :] = (ct_ref[rows, :].astype(jnp.float32) * conv).astype(jnp.bfloat16)
            gk_ref[rows, :] = (adj * v_ref[rows, :].astype(jnp.float32)).astype(jnp.bfloat16)
            gv_ref[rows, :] = (adj * k_ref[rows, :].astype(jnp.float32)).astype(jnp.bfloat16)
            sr = srev_ref[rows, :]
            zero = jnp.zeros_like(sr)
            a = jnp.concatenate([jnp.where(lo, sr, zero), jnp.where(lo, zero, sr)], 0)
            g = lax.dot_general(
                a, pw, (((1,), (1,)), ((), ())), preferred_element_type=jnp.float32
            )
            gsum = gsum + g * cmask
        d0 = pltpu.roll(gsum[:BLK], 0, 1, stride=1, stride_axis=0).sum(0, keepdims=True)
        d1 = pltpu.roll(gsum[BLK:], 0, 1, stride=1, stride_axis=0).sum(0, keepdims=True)
        gd_ref[0] = jnp.concatenate([d0, d1], 0)

    return kernel


def per_device(value_rows, key_rows, query_rows, cotangent, filter_taps, doc_blocks):
    tok_rows, channels = value_rows.shape
    filters, taps_total = filter_taps.shape
    nb = tok_rows // BLK
    reach = -(-taps_total // tok_rows)
    lags = taps_total // BLK + 1
    width = lags * BLK
    span = width + BLK
    base = (lags - 1) * BLK
    steps = channels // BLK
    product = (key_rows.astype(jnp.float32) * value_rows.astype(jnp.float32)).astype(jnp.bfloat16)
    scaled = (cotangent.astype(jnp.float32) * query_rows.astype(jnp.float32)).astype(jnp.bfloat16)
    earlier = [passed_along(product, "seq", d) for d in range(reach, 0, -1)]
    later = [passed_along(scaled, "seq", -d) for d in range(1, reach + 1)]
    pext = jnp.concatenate(earlier + [product], 0)
    sext = jnp.concatenate([scaled] + later, 0)
    srev = scaled.reshape(nb, BLK, channels)[:, ::-1].reshape(tok_rows, channels)
    own0 = reach * nb
    conv_start = (own0 - (lags - 1)) * BLK

    rounded = filter_taps.astype(jnp.bfloat16).astype(jnp.float32)
    k_idx = np.arange(span)
    qc = tap_rows(rounded, base + BLK - 1 - k_idx)
    qa = tap_rows(rounded, k_idx - BLK)

    nblk = doc_blocks.shape[0]
    margin = lags + nb
    padded = jnp.concatenate(
        [jnp.full((margin,), -1, jnp.int32), doc_blocks, jnp.full((margin,), -2, jnp.int32)], 0
    )
    shard = lax.axis_index("seq")
    window = lax.dynamic_slice_in_dim(padded, shard * nb + margin - (lags - 1), 2 * (lags - 1) + nb)
    own = jnp.stack([window[lags - 1 + n] for n in range(nb)])
    conv_docs = jnp.stack([window[n : n + lags] for n in range(nb)])
    adj_docs = jnp.stack([window[lags - 1 + n : lags - 1 + n + lags] for n in range(nb)])
    links = jnp.concatenate([conv_docs == own[:, None], adj_docs == own[:, None]], 0)
    cm = jnp.repeat(links.astype(jnp.float32), BLK, axis=1)

    ext_rows = pext.shape[0]
    whole = lambda shape: pl.BlockSpec(shape, lambda s: (0, 0))
    lanes = lambda r: pl.BlockSpec((r, BLK), lambda s: (0, s))
    kernel = make_kernel(nb, lags, width, span, conv_start)
    outs = pl.pallas_call(
        kernel,
        grid=(steps,),
        in_specs=[
            whole((filters, span)),
            whole((filters, span)),
            whole((2 * nb, width)),
            lanes(ext_rows),
            lanes(ext_rows),
            lanes(tok_rows),
            lanes(tok_rows),
            lanes(tok_rows),
            lanes(tok_rows),
            lanes(tok_rows),
        ],
        out_specs=[
            lanes(tok_rows),
            lanes(tok_rows),
            lanes(tok_rows),
            lanes(tok_rows),
            pl.BlockSpec((1, 2, width), lambda s: (s, 0, 0)),
        ],
        out_shape=[
            jax.ShapeDtypeStruct((tok_rows, channels), jnp.bfloat16),
            jax.ShapeDtypeStruct((tok_rows, channels), jnp.bfloat16),
            jax.ShapeDtypeStruct((tok_rows, channels), jnp.bfloat16),
            jax.ShapeDtypeStruct((tok_rows, channels), jnp.bfloat16),
            jax.ShapeDtypeStruct((steps, 2, width), jnp.float32),
        ],
        compiler_params=pltpu.CompilerParams(
            dimension_semantics=("arbitrary",), vmem_limit_bytes=48 * 1024 * 1024
        ),
    )(qc, qa, cm, pext, sext, srev, query_rows, cotangent, key_rows, value_rows)
    output_rows, grad_query, grad_key, grad_value, diag = outs
    diag = diag.reshape(filters, width)
    j_idx = base + BLK - 1 - np.arange(taps_total)
    taps_grad = tap_rows_any(diag, j_idx) * (1.0 / (tok_rows * lax.axis_size("seq")))
    grad_filter = lax.psum(taps_grad, ("seq", "head"))
    return (output_rows, grad_query, grad_key, grad_value, grad_filter)


def tap_rows_any(values, index):
    rows, cols = values.shape
    padded = jnp.concatenate([values, jnp.zeros((rows, 1), values.dtype)], 1)
    safe = np.where((index >= 0) & (index < cols), index, cols)
    return jnp.take(padded, jnp.asarray(safe, jnp.int32), axis=1)


def solution(mesh):
    in_specs = (P("seq", "head"), P("seq", "head"), P("seq", "head"), P("seq", "head"), P(), P())
    out_specs = (P("seq", "head"), P("seq", "head"), P("seq", "head"), P("seq", "head"), P())
    return jax.shard_map(
        per_device, mesh=mesh, in_specs=in_specs, out_specs=out_specs, check_vma=False
    )
```

profile of v0, /device:TPU:38, one launch (start us, length us, event | category | flops | bytes accessed | tf_op | source)
XLA Modules:
  0.0 360.8 jit_solution(11382696797662935264)
XLA Ops:
  7.2 1.4 multiply_convert_fusion.1
  8.6 4.3 %collective-permute-start = (bf16[256,1024]{1,0:T(8,128)(2,1)S(1)}, bf16[256,1024]{1,0:T(8,128)(2,1)}, u32[]{:S(2)}, u32[]{:S(2)}) collective-permute-start(bf16[256,1024]{1,0:T(8,128)(2,1)S(1)} %multiply_convert_fusion.1), channel_id=1, source_target_pairs={{0,32},{4,36},{8,40},{12,44},{16,48},{20,52},{24,56},{28,60},{32,6... | collective-permute-start | bytes 1572872 | tf_op jit(solution)/shard_map/ppermute | solution.py:16
  12.9 2.9 collective-permute-start.1
  15.8 2.4 collective-permute-start.2
  18.2 3.1 collective-permute-start.3
  21.3 4.1 %collective-permute-start.4 = (bf16[256,1024]{1,0:T(8,128)(2,1)S(1)}, bf16[256,1024]{1,0:T(8,128)(2,1)}, u32[]{:S(2)}, u32[]{:S(2)}) collective-permute-start(bf16[256,1024]{1,0:T(8,128)(2,1)S(1)} %multiply_convert_fusion.1), channel_id=1, source_target_pairs={{0,16},{4,20},{8,24},{12,28},{16,32},{20,36},{24,40},{28,44},{32,4... | collective-permute-start | bytes 1572872 | tf_op jit(solution)/shard_map/ppermute | solution.py:16
  27.4 2.3 constant_dynamic-update-slice_fusion.17
  31.5 3.9 %gather_fusion.1 = f32[2304,16]{1,0:T(8,128)S(1)} fusion(f32[16,2049]{0,1:T(8,128)S(1)} %copy.24, s32[3072]{0:T(1024)S(1)} %get-tuple-element.40), kind=kCustom, calls=%fused_computation.clone | custom fusion | bytes 304128 | tf_op jit(solution)/shard_map/jit(_take)/gather | solution.py:23
  35.7 3.9 %gather_fusion.2 = f32[2304,16]{1,0:T(8,128)S(1)} fusion(f32[16,2049]{0,1:T(8,128)S(1)} %copy.24, s32[3072]{0:T(1024)S(1)} %get-tuple-element.39), kind=kCustom, calls=%fused_computation.1.clone | custom fusion | bytes 304128 | tf_op jit(solution)/shard_map/jit(_take)/gather | solution.py:23
  40.7 24.9 %collective-permute-start.5 = (bf16[256,1024]{1,0:T(8,128)(2,1)S(1)}, bf16[256,1024]{1,0:T(8,128)(2,1)S(1)}, u32[]{:S(2)}, u32[]{:S(2)}) collective-permute-start(bf16[256,1024]{1,0:T(8,128)(2,1)S(1)} %multiply_convert_fusion.1), channel_id=1, source_target_pairs={{0,12},{4,16},{8,20},{12,24},{16,28},{20,32},{24,36},{28,40},{32,4... | collective-permute-start | bytes 1572872 | tf_op jit(solution)/shard_map/ppermute | solution.py:16
  66.7 5.9 %collective-permute-start.6 = (bf16[256,1024]{1,0:T(8,128)(2,1)S(1)}, bf16[256,1024]{1,0:T(8,128)(2,1)S(1)}, u32[]{:S(2)}, u32[]{:S(2)}) collective-permute-start(bf16[256,1024]{1,0:T(8,128)(2,1)S(1)} %multiply_convert_fusion.1), channel_id=1, source_target_pairs={{0,8},{4,12},{8,16},{12,20},{16,24},{20,28},{24,32},{28,36},{32,40... | collective-permute-start | bytes 1572872 | tf_op jit(solution)/shard_map/ppermute | solution.py:16
  72.6 1.1 constant_dynamic-update-slice_fusion.7
  73.7 1.9 collective-permute-start.7
  76.7 3.6 %collective-permute-start.8 = (bf16[256,1024]{1,0:T(8,128)(2,1)S(1)}, bf16[256,1024]{1,0:T(8,128)(2,1)S(1)}, u32[]{:S(2)}, u32[]{:S(2)}) collective-permute-start(bf16[256,1024]{1,0:T(8,128)(2,1)S(1)} %get-tuple-element.32), channel_id=1, source_target_pairs={{4,0},{8,4},{12,8},{16,12},{20,16},{24,20},{28,24},{32,28},{36,32}... | collective-permute-start | bytes 1572872 | tf_op jit(solution)/shard_map/ppermute | solution.py:16
  81.5 1.9 collective-permute-start.9
  83.4 1.1 constant_dynamic-update-slice_fusion.4
  84.5 1.9 collective-permute-start.10
  86.5 9.9 %collective-permute-done.6 = bf16[256,1024]{1,0:T(8,128)(2,1)S(1)} collective-permute-done((bf16[256,1024]{1,0:T(8,128)(2,1)S(1)}, bf16[256,1024]{1,0:T(8,128)(2,1)S(1)}, u32[]{:S(2)}, u32[]{:S(2)}) %collective-permute-start.6) | collective-permute-done | bytes 524320 | tf_op jit(solution)/shard_map/ppermute | solution.py:16
  96.4 1.9 collective-permute-start.11
  98.4 1.9 collective-permute-start.12
  100.5 2.3 collective-permute-start.13
  103.6 24.4 %collective-permute-done.9 = bf16[256,1024]{1,0:T(8,128)(2,1)S(1)} collective-permute-done((bf16[256,1024]{1,0:T(8,128)(2,1)S(1)}, bf16[256,1024]{1,0:T(8,128)(2,1)S(1)}, u32[]{:S(2)}, u32[]{:S(2)}) %collective-permute-start.9) | collective-permute-done | bytes 524320 | tf_op jit(solution)/shard_map/ppermute | solution.py:16
  128.0 1.3 collective-permute-start.14
  130.1 1.1 collective-permute-done.10
  131.3 1.3 collective-permute-start.15
  135.0 16.3 %collective-permute-done.13 = bf16[256,1024]{1,0:T(8,128)(2,1)S(1)} collective-permute-done((bf16[256,1024]{1,0:T(8,128)(2,1)S(1)}, bf16[256,1024]{1,0:T(8,128)(2,1)S(1)}, u32[]{:S(2)}, u32[]{:S(2)}) %collective-permute-start.13) | collective-permute-done | bytes 524320 | tf_op jit(solution)/shard_map/ppermute | solution.py:16
  152.2 4.6 %collective-permute-done.14 = bf16[256,1024]{1,0:T(8,128)(2,1)S(1)} collective-permute-done((bf16[256,1024]{1,0:T(8,128)(2,1)S(1)}, bf16[256,1024]{1,0:T(8,128)(2,1)S(1)}, u32[]{:S(2)}, u32[]{:S(2)}) %collective-permute-start.14) | collective-permute-done | bytes 524320 | tf_op jit(solution)/shard_map/ppermute | solution.py:16
  157.7 14.1 %collective-permute-done.15 = bf16[256,1024]{1,0:T(8,128)(2,1)S(1)} collective-permute-done((bf16[256,1024]{1,0:T(8,128)(2,1)S(1)}, bf16[256,1024]{1,0:T(8,128)(2,1)S(1)}, u32[]{:S(2)}, u32[]{:S(2)}) %collective-permute-start.15) | collective-permute-done | bytes 524320 | tf_op jit(solution)/shard_map/ppermute | solution.py:16
  172.7 26.5 %shard_map.128 = (bf16[256,1024]{1,0:T(8,128)(2,1)}, bf16[256,1024]{1,0:T(8,128)(2,1)}, bf16[256,1024]{1,0:T(8,128)(2,1)}, bf16[256,1024]{1,0:T(8,128)(2,1)}, f32[8,2,2176]{2,1,0:T(2,128)S(1)}) custom-call(f32[16,2304]{1,0:T(8,128)S(1)} %bitcast.20, f32[16,2304]{1,0:T(8,128)S(1)} %bitcast.21, f32[4,2176]{1,0:T(4,128)S(1)} %bitcast.22, ...), custom_call_target="tpu_custom_call" | custom-call | tf_op jit(solution)/shard_map/pallas_call | solution.py:117
  199.7 5.5 %gather_fusion = f32[2048,16]{1,0:T(8,128)S(1)} fusion(f32[16,2177]{0,1:T(8,128)S(1)} %concatenate.27, s32[2048]{0:T(1024)S(1)} %broadcast_clamp_fusion), kind=kCustom, calls=%fused_computation.2 | custom fusion | bytes 270336 | tf_op jit(solution)/shard_map/jit(_take)/gather | solution.py:162
  206.3 145.5 %all-reduce.4.cloned.1.call-done = f32[16,2048]{0,1:T(8,128)} async-done(((f32[16,2048]{0,1:T(8,128)}), f32[16,2048]{0,1:T(8,128)}) %all-reduce.4.cloned.1.call-update) | async-done | bytes 131088 | tf_op jit(solution)/shard_map/psum | solution.py:154
  351.8 2.2 copy.29
  (59 shorter events, 17.0 us)
Async XLA Ops:
  7.2 344.6 %all-reduce.4.cloned.1.call-start = ((), (), s32[]{:S(2)}) async-start(), calls=%async_computation | async-start | bytes 2097152 | tf_op jit(solution)/shard_map/psum | solution.py:154
  8.6 32.1 %collective-permute-start = (bf16[256,1024]{1,0:T(8,128)(2,1)S(1)}, bf16[256,1024]{1,0:T(8,128)(2,1)}, u32[]{:S(2)}, u32[]{:S(2)}) collective-permute-start(bf16[256,1024]{1,0:T(8,128)(2,1)S(1)} %multiply_convert_fusion.1), channel_id=1, source_target_pairs={{0,32},{4,36},{8,40},{12,44},{16,48},{20,52},{24,56},{28,60},{32,6... | collective-permute-start | bytes 1572872 | tf_op jit(solution)/shard_map/ppermute | solution.py:16
  12.9 53.8 %collective-permute-start.1 = (bf16[256,1024]{1,0:T(8,128)(2,1)S(1)}, bf16[256,1024]{1,0:T(8,128)(2,1)}, u32[]{:S(2)}, u32[]{:S(2)}) collective-permute-start(bf16[256,1024]{1,0:T(8,128)(2,1)S(1)} %multiply_convert_fusion.1), channel_id=1, source_target_pairs={{0,28},{4,32},{8,36},{12,40},{16,44},{20,48},{24,52},{28,56},{32,6... | collective-permute-start | bytes 1572872 | tf_op jit(solution)/shard_map/ppermute | solution.py:16
  15.8 57.9 %collective-permute-start.2 = (bf16[256,1024]{1,0:T(8,128)(2,1)S(1)}, bf16[256,1024]{1,0:T(8,128)(2,1)}, u32[]{:S(2)}, u32[]{:S(2)}) collective-permute-start(bf16[256,1024]{1,0:T(8,128)(2,1)S(1)} %multiply_convert_fusion.1), channel_id=1, source_target_pairs={{0,24},{4,28},{8,32},{12,36},{16,40},{20,44},{24,48},{28,52},{32,5... | collective-permute-start | bytes 1572872 | tf_op jit(solution)/shard_map/ppermute | solution.py:16
  18.2 58.5 %collective-permute-start.3 = (bf16[256,1024]{1,0:T(8,128)(2,1)S(1)}, bf16[256,1024]{1,0:T(8,128)(2,1)}, u32[]{:S(2)}, u32[]{:S(2)}) collective-permute-start(bf16[256,1024]{1,0:T(8,128)(2,1)S(1)} %multiply_convert_fusion.1), channel_id=1, source_target_pairs={{0,20},{4,24},{8,28},{12,32},{16,36},{20,40},{24,44},{28,48},{32,5... | collective-permute-start | bytes 1572872 | tf_op jit(solution)/shard_map/ppermute | solution.py:16
  21.3 60.2 %collective-permute-start.4 = (bf16[256,1024]{1,0:T(8,128)(2,1)S(1)}, bf16[256,1024]{1,0:T(8,128)(2,1)}, u32[]{:S(2)}, u32[]{:S(2)}) collective-permute-start(bf16[256,1024]{1,0:T(8,128)(2,1)S(1)} %multiply_convert_fusion.1), channel_id=1, source_target_pairs={{0,16},{4,20},{8,24},{12,28},{16,32},{20,36},{24,40},{28,44},{32,4... | collective-permute-start | bytes 1572872 | tf_op jit(solution)/shard_map/ppermute | solution.py:16
  40.7 43.8 %collective-permute-start.5 = (bf16[256,1024]{1,0:T(8,128)(2,1)S(1)}, bf16[256,1024]{1,0:T(8,128)(2,1)S(1)}, u32[]{:S(2)}, u32[]{:S(2)}) collective-permute-start(bf16[256,1024]{1,0:T(8,128)(2,1)S(1)} %multiply_convert_fusion.1), channel_id=1, source_target_pairs={{0,12},{4,16},{8,20},{12,24},{16,28},{20,32},{24,36},{28,40},{32,4... | collective-permute-start | bytes 1572872 | tf_op jit(solution)/shard_map/ppermute | solution.py:16
  66.7 29.7 %collective-permute-start.6 = (bf16[256,1024]{1,0:T(8,128)(2,1)S(1)}, bf16[256,1024]{1,0:T(8,128)(2,1)S(1)}, u32[]{:S(2)}, u32[]{:S(2)}) collective-permute-start(bf16[256,1024]{1,0:T(8,128)(2,1)S(1)} %multiply_convert_fusion.1), channel_id=1, source_target_pairs={{0,8},{4,12},{8,16},{12,20},{16,24},{20,28},{24,32},{28,36},{32,40... | collective-permute-start | bytes 1572872 | tf_op jit(solution)/shard_map/ppermute | solution.py:16
  73.7 24.7 %collective-permute-start.7 = (bf16[256,1024]{1,0:T(8,128)(2,1)S(1)}, bf16[256,1024]{1,0:T(8,128)(2,1)S(1)}, u32[]{:S(2)}, u32[]{:S(2)}) collective-permute-start(bf16[256,1024]{1,0:T(8,128)(2,1)S(1)} %multiply_convert_fusion.1), channel_id=1, source_target_pairs={{0,4},{4,8},{8,12},{12,16},{16,20},{20,24},{24,28},{28,32},{32,36}... | collective-permute-start | bytes 1572872 | tf_op jit(solution)/shard_map/ppermute | solution.py:16
  76.7 23.7 %collective-permute-start.8 = (bf16[256,1024]{1,0:T(8,128)(2,1)S(1)}, bf16[256,1024]{1,0:T(8,128)(2,1)S(1)}, u32[]{:S(2)}, u32[]{:S(2)}) collective-permute-start(bf16[256,1024]{1,0:T(8,128)(2,1)S(1)} %get-tuple-element.32), channel_id=1, source_target_pairs={{4,0},{8,4},{12,8},{16,12},{20,16},{24,20},{28,24},{32,28},{36,32}... | collective-permute-start | bytes 1572872 | tf_op jit(solution)/shard_map/ppermute | solution.py:16
  81.5 46.5 %collective-permute-start.9 = (bf16[256,1024]{1,0:T(8,128)(2,1)S(1)}, bf16[256,1024]{1,0:T(8,128)(2,1)S(1)}, u32[]{:S(2)}, u32[]{:S(2)}) collective-permute-start(bf16[256,1024]{1,0:T(8,128)(2,1)S(1)} %get-tuple-element.32), channel_id=1, source_target_pairs={{8,0},{12,4},{16,8},{20,12},{24,16},{28,20},{32,24},{36,28},{40,32... | collective-permute-start | bytes 1572872 | tf_op jit(solution)/shard_map/ppermute | solution.py:16
  84.5 46.8 %collective-permute-start.10 = (bf16[256,1024]{1,0:T(8,128)(2,1)S(1)}, bf16[256,1024]{1,0:T(8,128)(2,1)S(1)}, u32[]{:S(2)}, u32[]{:S(2)}) collective-permute-start(bf16[256,1024]{1,0:T(8,128)(2,1)S(1)} %get-tuple-element.32), channel_id=1, source_target_pairs={{12,0},{16,4},{20,8},{24,12},{28,16},{32,20},{36,24},{40,28},{44,3... | collective-permute-start | bytes 1572872 | tf_op jit(solution)/shard_map/ppermute | solution.py:16
  96.4 37.0 %collective-permute-start.11 = (bf16[256,1024]{1,0:T(8,128)(2,1)S(1)}, bf16[256,1024]{1,0:T(8,128)(2,1)S(1)}, u32[]{:S(2)}, u32[]{:S(2)}) collective-permute-start(bf16[256,1024]{1,0:T(8,128)(2,1)S(1)} %get-tuple-element.32), channel_id=1, source_target_pairs={{16,0},{20,4},{24,8},{28,12},{32,16},{36,20},{40,24},{44,28},{48,3... | collective-permute-start | bytes 1572872 | tf_op jit(solution)/shard_map/ppermute | solution.py:16
  98.4 35.8 %collective-permute-start.12 = (bf16[256,1024]{1,0:T(8,128)(2,1)S(1)}, bf16[256,1024]{1,0:T(8,128)(2,1)S(1)}, u32[]{:S(2)}, u32[]{:S(2)}) collective-permute-start(bf16[256,1024]{1,0:T(8,128)(2,1)S(1)} %get-tuple-element.32), channel_id=1, source_target_pairs={{20,0},{24,4},{28,8},{32,12},{36,16},{40,20},{44,24},{48,28},{52,3... | collective-permute-start | bytes 1572872 | tf_op jit(solution)/shard_map/ppermute | solution.py:16
  100.3 72.3 %copy-start = (bf16[256,1024]{1,0:T(8,128)(2,1)S(1)}, bf16[256,1024]{1,0:T(8,128)(2,1)}, u32[]{:S(2)}) copy-start(bf16[256,1024]{1,0:T(8,128)(2,1)} %v_ref.1) | copy-start | bytes 1572868
  100.4 72.3 %copy-start.1 = (bf16[256,1024]{1,0:T(8,128)(2,1)S(1)}, bf16[256,1024]{1,0:T(8,128)(2,1)}, u32[]{:S(2)}) copy-start(bf16[256,1024]{1,0:T(8,128)(2,1)} %k_ref.1) | copy-start | bytes 1572868
  100.4 72.3 %copy-start.2 = (bf16[256,1024]{1,0:T(8,128)(2,1)S(1)}, bf16[256,1024]{1,0:T(8,128)(2,1)}, u32[]{:S(2)}) copy-start(bf16[256,1024]{1,0:T(8,128)(2,1)} %q_ref.1) | copy-start | bytes 1572868
  100.4 72.3 %copy-start.3 = (bf16[256,1024]{1,0:T(8,128)(2,1)S(1)}, bf16[256,1024]{1,0:T(8,128)(2,1)}, u32[]{:S(2)}) copy-start(bf16[256,1024]{1,0:T(8,128)(2,1)} %ct_ref.1) | copy-start | bytes 1572868
  100.4 72.2 %copy-start.4 = (bf16[2304,1024]{1,0:T(8,128)(2,1)}, bf16[2304,1024]{1,0:T(8,128)(2,1)S(1)}, u32[]{:S(2)}) copy-start(bf16[2304,1024]{1,0:T(8,128)(2,1)S(1)} %constant_dynamic-update-slice_fusion.pext_ref) | copy-start | bytes 14155780
  100.5 50.9 %collective-permute-start.13 = (bf16[256,1024]{1,0:T(8,128)(2,1)S(1)}, bf16[256,1024]{1,0:T(8,128)(2,1)S(1)}, u32[]{:S(2)}, u32[]{:S(2)}) collective-permute-start(bf16[256,1024]{1,0:T(8,128)(2,1)S(1)} %get-tuple-element.32), channel_id=1, source_target_pairs={{24,0},{28,4},{32,8},{36,12},{40,16},{44,20},{48,24},{52,28},{56,3... | collective-permute-start | bytes 1572872 | tf_op jit(solution)/shard_map/ppermute | solution.py:16
  128.0 28.9 %collective-permute-start.14 = (bf16[256,1024]{1,0:T(8,128)(2,1)S(1)}, bf16[256,1024]{1,0:T(8,128)(2,1)S(1)}, u32[]{:S(2)}, u32[]{:S(2)}) collective-permute-start(bf16[256,1024]{1,0:T(8,128)(2,1)S(1)} %get-tuple-element.32), channel_id=1, source_target_pairs={{28,0},{32,4},{36,8},{40,12},{44,16},{48,20},{52,24},{56,28},{60,3... | collective-permute-start | bytes 1572872 | tf_op jit(solution)/shard_map/ppermute | solution.py:16
  131.3 40.6 %collective-permute-start.15 = (bf16[256,1024]{1,0:T(8,128)(2,1)S(1)}, bf16[256,1024]{1,0:T(8,128)(2,1)S(1)}, u32[]{:S(2)}, u32[]{:S(2)}) collective-permute-start(bf16[256,1024]{1,0:T(8,128)(2,1)S(1)} %get-tuple-element.32), channel_id=1, source_target_pairs={{32,0},{36,4},{40,8},{44,12},{48,16},{52,20},{56,24},{60,28},{64,3... | collective-permute-start | bytes 1572872 | tf_op jit(solution)/shard_map/ppermute | solution.py:16
Sparse Core Ops, SparseCore 0:
  206.4 145.3 all-reduce.3
where the time goes:
time: 365 us; the launch traced here: 361 us
  waiting for transfers between devices  216 us (59%)
  starting transfers between devices  65.7 us (18%)
  local copies, waits for them, and re-layouts  30.4 us (8%)
  Pallas kernels  26.5 us (7%)
  between operations  14.4 us (4%)
  other arithmetic  7.87 us (2%)
    psum x1, waiting for transfers between devices, per_device(): grad_filter = lax.psum(taps_grad, ('seq', 'head'))  146 us
    ppermute x16, waiting for transfers between devices, passed_along(): return lax.ppermute(value, axis, pairs)  70.5 us
    ppermute x16, starting transfers between devices, passed_along(): return lax.ppermute(value, axis, pairs)  65.7 us
    pallas_call x1, Pallas kernels, per_device(): pl.pallas_call(kernel, grid=(steps,), in_specs=[whole((filters, span)), w...  26.5 us
    unnamed x28, local copies, waits for them, and re-layouts  13.8 us
    gather x4, local copies, waits for them, and re-layouts, tap_rows(): return jnp.take(padded, jnp.asarray(safe, jnp.int32), axis=1)  8.47 us
  transfers between devices with their start and end apart: 17, of which 7 were waited for; matrix products, arithmetic and copies ran while one was open for 7% of the time, Pallas kernels for 0%

commit v1 on v0

--- a/solution.py
+++ b/solution.py
@@ -151,8 +151,19 @@
     diag = diag.reshape(filters, width)
     j_idx = base + BLK - 1 - np.arange(taps_total)
     taps_grad = tap_rows_any(diag, j_idx) * (1.0 / (tok_rows * lax.axis_size("seq")))
-    grad_filter = lax.psum(taps_grad, ("seq", "head"))
+    grad_filter = doubled_total(taps_grad, ("head", "seq"))
     return (output_rows, grad_query, grad_key, grad_value, grad_filter)
+
+
+def doubled_total(value, axes):
+    for axis in axes:
+        length = lax.axis_size(axis)
+        bit = 1
+        while bit < length:
+            pairs = [(i, i ^ bit) for i in range(length)]
+            value = value + lax.ppermute(value, axis, pairs)
+            bit *= 2
+    return value
 
 
 def tap_rows_any(values, index):

time: 365 us -> 240 us (0.66)
  waiting for transfers between devices: 216 us -> 107 us
  between operations: 14.4 us -> 1.09 us
    psum x1 -> x0, waiting for transfers between devices: 146 us -> none  [per_device(): grad_filter = lax.psum(taps_grad, ('seq', 'head'))]
    ppermute x0 -> x7, waiting for transfers between devices: none -> 36.9 us  [doubled_total(): value = value + lax.ppermute(value, axis, pairs)]
    unnamed x28 -> x27, local copies, waits for them, and re-layouts: 13.8 us -> 11.6 us
  transfers between devices with their start and end apart: 17 -> 23, of which waited for: 7 -> 13; matrix products, arithmetic and copies ran while one was open for 7% -> 11% of each run, Pallas kernels for 0% -> 0%
where the time goes in v1:
time: 240 us; the launch traced here: 239 us
  waiting for transfers between devices  107 us (45%)
  starting transfers between devices  68 us (28%)
  local copies, waits for them, and re-layouts  28.5 us (12%)
  Pallas kernels  26.5 us (11%)
  other arithmetic  7.56 us (3%)
    ppermute x16, waiting for transfers between devices, passed_along(): return lax.ppermute(value, axis, pairs)  70.4 us
    ppermute x16, starting transfers between devices, passed_along(): return lax.ppermute(value, axis, pairs)  65.7 us
    ppermute x7, waiting for transfers between devices, doubled_total(): value = value + lax.ppermute(value, axis, pairs)  36.9 us
    pallas_call x1, Pallas kernels, per_device(): pl.pallas_call(kernel, grid=(steps,), in_specs=[whole((filters, span)), w...  26.5 us
    unnamed x27, local copies, waits for them, and re-layouts  11.6 us
    gather x4, local copies, waits for them, and re-layouts, tap_rows(): return jnp.take(padded, jnp.asarray(safe, jnp.int32), axis=1)  8.47 us
    gather x2, local copies, waits for them, and re-layouts, tap_rows_any(): return jnp.take(padded, jnp.asarray(safe, jnp.int32), axis=1)  5.77 us
  transfers between devices with their start and end apart: 23, of which 13 were waited for; matrix products, arithmetic and copies ran while one was open for 11% of the time, Pallas kernels for 0%

profile of v1, /device:TPU:38, one launch (start us, length us, event | category | flops | bytes accessed | tf_op | source)
XLA Modules:
  0.0 239.0 jit_solution(11471811987112221503)
XLA Ops:
  0.6 1.4 multiply_convert_fusion.1
  2.0 4.3 %collective-permute-start = (bf16[256,1024]{1,0:T(8,128)(2,1)S(1)}, bf16[256,1024]{1,0:T(8,128)(2,1)}, u32[]{:S(2)}, u32[]{:S(2)}) collective-permute-start(bf16[256,1024]{1,0:T(8,128)(2,1)S(1)} %multiply_convert_fusion.1), channel_id=1, source_target_pairs={{0,32},{4,36},{8,40},{12,44},{16,48},{20,52},{24,56},{28,60},{32,6... | collective-permute-start | bytes 1572872 | tf_op jit(solution)/shard_map/ppermute | solution.py:16
  6.3 2.9 %collective-permute-start.1 = (bf16[256,1024]{1,0:T(8,128)(2,1)S(1)}, bf16[256,1024]{1,0:T(8,128)(2,1)}, u32[]{:S(2)}, u32[]{:S(2)}) collective-permute-start(bf16[256,1024]{1,0:T(8,128)(2,1)S(1)} %multiply_convert_fusion.1), channel_id=1, source_target_pairs={{0,28},{4,32},{8,36},{12,40},{16,44},{20,48},{24,52},{28,56},{32,6... | collective-permute-start | bytes 1572872 | tf_op jit(solution)/shard_map/ppermute | solution.py:16
  9.3 2.4 collective-permute-start.2
  11.6 3.1 %collective-permute-start.3 = (bf16[256,1024]{1,0:T(8,128)(2,1)S(1)}, bf16[256,1024]{1,0:T(8,128)(2,1)}, u32[]{:S(2)}, u32[]{:S(2)}) collective-permute-start(bf16[256,1024]{1,0:T(8,128)(2,1)S(1)} %multiply_convert_fusion.1), channel_id=1, source_target_pairs={{0,20},{4,24},{8,28},{12,32},{16,36},{20,40},{24,44},{28,48},{32,5... | collective-permute-start | bytes 1572872 | tf_op jit(solution)/shard_map/ppermute | solution.py:16
  14.7 4.1 %collective-permute-start.4 = (bf16[256,1024]{1,0:T(8,128)(2,1)S(1)}, bf16[256,1024]{1,0:T(8,128)(2,1)}, u32[]{:S(2)}, u32[]{:S(2)}) collective-permute-start(bf16[256,1024]{1,0:T(8,128)(2,1)S(1)} %multiply_convert_fusion.1), channel_id=1, source_target_pairs={{0,16},{4,20},{8,24},{12,28},{16,32},{20,36},{24,40},{28,44},{32,4... | collective-permute-start | bytes 1572872 | tf_op jit(solution)/shard_map/ppermute | solution.py:16
  20.8 2.2 constant_dynamic-update-slice_fusion.17
  24.8 3.9 %gather_fusion.1 = f32[2304,16]{1,0:T(8,128)S(1)} fusion(f32[16,2049]{0,1:T(8,128)S(1)} %copy.43, s32[3072]{0:T(1024)S(1)} %get-tuple-element.40), kind=kCustom, calls=%fused_computation.clone | custom fusion | bytes 304128 | tf_op jit(solution)/shard_map/jit(_take)/gather | solution.py:23
  29.1 3.9 %gather_fusion.2 = f32[2304,16]{1,0:T(8,128)S(1)} fusion(f32[16,2049]{0,1:T(8,128)S(1)} %copy.43, s32[3072]{0:T(1024)S(1)} %get-tuple-element.39), kind=kCustom, calls=%fused_computation.1.clone | custom fusion | bytes 304128 | tf_op jit(solution)/shard_map/jit(_take)/gather | solution.py:23
  34.0 24.9 %collective-permute-start.5 = (bf16[256,1024]{1,0:T(8,128)(2,1)S(1)}, bf16[256,1024]{1,0:T(8,128)(2,1)S(1)}, u32[]{:S(2)}, u32[]{:S(2)}) collective-permute-start(bf16[256,1024]{1,0:T(8,128)(2,1)S(1)} %multiply_convert_fusion.1), channel_id=1, source_target_pairs={{0,12},{4,16},{8,20},{12,24},{16,28},{20,32},{24,36},{28,40},{32,4... | collective-permute-start | bytes 1572872 | tf_op jit(solution)/shard_map/ppermute | solution.py:16
  60.1 5.9 %collective-permute-start.6 = (bf16[256,1024]{1,0:T(8,128)(2,1)S(1)}, bf16[256,1024]{1,0:T(8,128)(2,1)S(1)}, u32[]{:S(2)}, u32[]{:S(2)}) collective-permute-start(bf16[256,1024]{1,0:T(8,128)(2,1)S(1)} %multiply_convert_fusion.1), channel_id=1, source_target_pairs={{0,8},{4,12},{8,16},{12,20},{16,24},{20,28},{24,32},{28,36},{32,40... | collective-permute-start | bytes 1572872 | tf_op jit(solution)/shard_map/ppermute | solution.py:16
  67.1 1.9 collective-permute-start.7
  70.1 3.6 %collective-permute-start.8 = (bf16[256,1024]{1,0:T(8,128)(2,1)S(1)}, bf16[256,1024]{1,0:T(8,128)(2,1)S(1)}, u32[]{:S(2)}, u32[]{:S(2)}) collective-permute-start(bf16[256,1024]{1,0:T(8,128)(2,1)S(1)} %get-tuple-element.32), channel_id=1, source_target_pairs={{4,0},{8,4},{12,8},{16,12},{20,16},{24,20},{28,24},{32,28},{36,32}... | collective-permute-start | bytes 1572872 | tf_op jit(solution)/shard_map/ppermute | solution.py:16
  74.9 1.9 collective-permute-start.9
  77.9 1.9 collective-permute-start.10
  79.9 9.9 %collective-permute-done.6 = bf16[256,1024]{1,0:T(8,128)(2,1)S(1)} collective-permute-done((bf16[256,1024]{1,0:T(8,128)(2,1)S(1)}, bf16[256,1024]{1,0:T(8,128)(2,1)S(1)}, u32[]{:S(2)}, u32[]{:S(2)}) %collective-permute-start.6) | collective-permute-done | bytes 524320 | tf_op jit(solution)/shard_map/ppermute | solution.py:16
  89.8 1.9 collective-permute-start.11
  91.8 1.9 collective-permute-start.12
  93.9 2.3 collective-permute-start.13
  97.1 24.4 %collective-permute-done.9 = bf16[256,1024]{1,0:T(8,128)(2,1)S(1)} collective-permute-done((bf16[256,1024]{1,0:T(8,128)(2,1)S(1)}, bf16[256,1024]{1,0:T(8,128)(2,1)S(1)}, u32[]{:S(2)}, u32[]{:S(2)}) %collective-permute-start.9) | collective-permute-done | bytes 524320 | tf_op jit(solution)/shard_map/ppermute | solution.py:16
  128.5 16.3 %collective-permute-done.13 = bf16[256,1024]{1,0:T(8,128)(2,1)S(1)} collective-permute-done((bf16[256,1024]{1,0:T(8,128)(2,1)S(1)}, bf16[256,1024]{1,0:T(8,128)(2,1)S(1)}, u32[]{:S(2)}, u32[]{:S(2)}) %collective-permute-start.13) | collective-permute-done | bytes 524320 | tf_op jit(solution)/shard_map/ppermute | solution.py:16
  145.6 4.6 %collective-permute-done.14 = bf16[256,1024]{1,0:T(8,128)(2,1)S(1)} collective-permute-done((bf16[256,1024]{1,0:T(8,128)(2,1)S(1)}, bf16[256,1024]{1,0:T(8,128)(2,1)S(1)}, u32[]{:S(2)}, u32[]{:S(2)}) %collective-permute-start.14) | collective-permute-done | bytes 524320 | tf_op jit(solution)/shard_map/ppermute | solution.py:16
  151.2 14.1 %collective-permute-done.15 = bf16[256,1024]{1,0:T(8,128)(2,1)S(1)} collective-permute-done((bf16[256,1024]{1,0:T(8,128)(2,1)S(1)}, bf16[256,1024]{1,0:T(8,128)(2,1)S(1)}, u32[]{:S(2)}, u32[]{:S(2)}) %collective-permute-start.15) | collective-permute-done | bytes 524320 | tf_op jit(solution)/shard_map/ppermute | solution.py:16
  166.1 26.5 %shard_map.128 = (bf16[256,1024]{1,0:T(8,128)(2,1)}, bf16[256,1024]{1,0:T(8,128)(2,1)}, bf16[256,1024]{1,0:T(8,128)(2,1)}, bf16[256,1024]{1,0:T(8,128)(2,1)}, f32[8,2,2176]{2,1,0:T(2,128)S(1)}) custom-call(f32[16,2304]{1,0:T(8,128)S(1)} %bitcast.22, f32[16,2304]{1,0:T(8,128)S(1)} %bitcast.23, f32[4,2176]{1,0:T(4,128)S(1)} %bitcast.24, ...), custom_call_target="tpu_custom_call" | custom-call | tf_op jit(solution)/shard_map/pallas_call | solution.py:117
  193.1 5.5 %gather_fusion = f32[2048,16]{1,0:T(8,128)S(1)} fusion(f32[16,2177]{0,1:T(8,128)S(1)} %concatenate.27, s32[2048]{0:T(1024)S(1)} %broadcast_clamp_fusion), kind=kCustom, calls=%fused_computation.2 | custom fusion | bytes 270336 | tf_op jit(solution)/shard_map/jit(_take)/gather | solution.py:173
  199.1 6.2 %collective-permute-done.16 = f32[16,2048]{1,0:T(8,128)S(1)} collective-permute-done((f32[16,2048]{1,0:T(8,128)S(1)}, f32[16,2048]{1,0:T(8,128)S(1)}, u32[]{:S(2)}, u32[]{:S(2)}) %collective-permute-start.16) | collective-permute-done | bytes 131104 | tf_op jit(solution)/shard_map/ppermute | solution.py:164
  205.4 1.7 collective-permute-start.17
  207.1 4.9 %collective-permute-done.17 = f32[16,2048]{1,0:T(8,128)S(1)} collective-permute-done((f32[16,2048]{1,0:T(8,128)S(1)}, f32[16,2048]{1,0:T(8,128)S(1)}, u32[]{:S(2)}, u32[]{:S(2)}) %collective-permute-start.17) | collective-permute-done | bytes 131104 | tf_op jit(solution)/shard_map/ppermute | solution.py:164
  213.5 5.5 %collective-permute-done.19 = f32[16,2048]{1,0:T(8,128)S(1)} collective-permute-done((f32[16,2048]{1,0:T(8,128)S(1)}, f32[16,2048]{1,0:T(8,128)S(1)}, u32[]{:S(2)}, u32[]{:S(2)}) %collective-permute-start.19) | collective-permute-done | bytes 131104 | tf_op jit(solution)/shard_map/ppermute | solution.py:164
  219.2 6.5 %collective-permute-done.20 = f32[16,2048]{1,0:T(8,128)S(1)} collective-permute-done((f32[16,2048]{1,0:T(8,128)S(1)}, f32[16,2048]{1,0:T(8,128)S(1)}, u32[]{:S(2)}, u32[]{:S(2)}) %collective-permute-start.20) | collective-permute-done | bytes 131104 | tf_op jit(solution)/shard_map/ppermute | solution.py:164
  225.7 6.0 %collective-permute-done.21 = f32[16,2048]{1,0:T(8,128)S(1)} collective-permute-done((f32[16,2048]{1,0:T(8,128)S(1)}, f32[16,2048]{1,0:T(8,128)S(1)}, u32[]{:S(2)}, u32[]{:S(2)}) %collective-permute-start.21) | collective-permute-done | bytes 131104 | tf_op jit(solution)/shard_map/ppermute | solution.py:164
  231.8 6.5 %collective-permute-done.22 = f32[16,2048]{1,0:T(8,128)S(1)} collective-permute-done((f32[16,2048]{1,0:T(8,128)S(1)}, f32[16,2048]{1,0:T(8,128)S(1)}, u32[]{:S(2)}, u32[]{:S(2)}) %collective-permute-start.22) | collective-permute-done | bytes 131104 | tf_op jit(solution)/shard_map/ppermute | solution.py:164
  (77 shorter events, 24.8 us)
Async XLA Ops:
  2.0 32.0 %collective-permute-start = (bf16[256,1024]{1,0:T(8,128)(2,1)S(1)}, bf16[256,1024]{1,0:T(8,128)(2,1)}, u32[]{:S(2)}, u32[]{:S(2)}) collective-permute-start(bf16[256,1024]{1,0:T(8,128)(2,1)S(1)} %multiply_convert_fusion.1), channel_id=1, source_target_pairs={{0,32},{4,36},{8,40},{12,44},{16,48},{20,52},{24,56},{28,60},{32,6... | collective-permute-start | bytes 1572872 | tf_op jit(solution)/shard_map/ppermute | solution.py:16
  6.3 53.8 %collective-permute-start.1 = (bf16[256,1024]{1,0:T(8,128)(2,1)S(1)}, bf16[256,1024]{1,0:T(8,128)(2,1)}, u32[]{:S(2)}, u32[]{:S(2)}) collective-permute-start(bf16[256,1024]{1,0:T(8,128)(2,1)S(1)} %multiply_convert_fusion.1), channel_id=1, source_target_pairs={{0,28},{4,32},{8,36},{12,40},{16,44},{20,48},{24,52},{28,56},{32,6... | collective-permute-start | bytes 1572872 | tf_op jit(solution)/shard_map/ppermute | solution.py:16
  9.3 57.9 %collective-permute-start.2 = (bf16[256,1024]{1,0:T(8,128)(2,1)S(1)}, bf16[256,1024]{1,0:T(8,128)(2,1)}, u32[]{:S(2)}, u32[]{:S(2)}) collective-permute-start(bf16[256,1024]{1,0:T(8,128)(2,1)S(1)} %multiply_convert_fusion.1), channel_id=1, source_target_pairs={{0,24},{4,28},{8,32},{12,36},{16,40},{20,44},{24,48},{28,52},{32,5... | collective-permute-start | bytes 1572872 | tf_op jit(solution)/shard_map/ppermute | solution.py:16
  11.6 58.5 %collective-permute-start.3 = (bf16[256,1024]{1,0:T(8,128)(2,1)S(1)}, bf16[256,1024]{1,0:T(8,128)(2,1)}, u32[]{:S(2)}, u32[]{:S(2)}) collective-permute-start(bf16[256,1024]{1,0:T(8,128)(2,1)S(1)} %multiply_convert_fusion.1), channel_id=1, source_target_pairs={{0,20},{4,24},{8,28},{12,32},{16,36},{20,40},{24,44},{28,48},{32,5... | collective-permute-start | bytes 1572872 | tf_op jit(solution)/shard_map/ppermute | solution.py:16
  14.7 60.2 %collective-permute-start.4 = (bf16[256,1024]{1,0:T(8,128)(2,1)S(1)}, bf16[256,1024]{1,0:T(8,128)(2,1)}, u32[]{:S(2)}, u32[]{:S(2)}) collective-permute-start(bf16[256,1024]{1,0:T(8,128)(2,1)S(1)} %multiply_convert_fusion.1), channel_id=1, source_target_pairs={{0,16},{4,20},{8,24},{12,28},{16,32},{20,36},{24,40},{28,44},{32,4... | collective-permute-start | bytes 1572872 | tf_op jit(solution)/shard_map/ppermute | solution.py:16
  34.0 43.8 %collective-permute-start.5 = (bf16[256,1024]{1,0:T(8,128)(2,1)S(1)}, bf16[256,1024]{1,0:T(8,128)(2,1)S(1)}, u32[]{:S(2)}, u32[]{:S(2)}) collective-permute-start(bf16[256,1024]{1,0:T(8,128)(2,1)S(1)} %multiply_convert_fusion.1), channel_id=1, source_target_pairs={{0,12},{4,16},{8,20},{12,24},{16,28},{20,32},{24,36},{28,40},{32,4... | collective-permute-start | bytes 1572872 | tf_op jit(solution)/shard_map/ppermute | solution.py:16
  60.1 29.7 %collective-permute-start.6 = (bf16[256,1024]{1,0:T(8,128)(2,1)S(1)}, bf16[256,1024]{1,0:T(8,128)(2,1)S(1)}, u32[]{:S(2)}, u32[]{:S(2)}) collective-permute-start(bf16[256,1024]{1,0:T(8,128)(2,1)S(1)} %multiply_convert_fusion.1), channel_id=1, source_target_pairs={{0,8},{4,12},{8,16},{12,20},{16,24},{20,28},{24,32},{28,36},{32,40... | collective-permute-start | bytes 1572872 | tf_op jit(solution)/shard_map/ppermute | solution.py:16
  67.1 24.7 %collective-permute-start.7 = (bf16[256,1024]{1,0:T(8,128)(2,1)S(1)}, bf16[256,1024]{1,0:T(8,128)(2,1)S(1)}, u32[]{:S(2)}, u32[]{:S(2)}) collective-permute-start(bf16[256,1024]{1,0:T(8,128)(2,1)S(1)} %multiply_convert_fusion.1), channel_id=1, source_target_pairs={{0,4},{4,8},{8,12},{12,16},{16,20},{20,24},{24,28},{28,32},{32,36}... | collective-permute-start | bytes 1572872 | tf_op jit(solution)/shard_map/ppermute | solution.py:16
  70.1 23.7 %collective-permute-start.8 = (bf16[256,1024]{1,0:T(8,128)(2,1)S(1)}, bf16[256,1024]{1,0:T(8,128)(2,1)S(1)}, u32[]{:S(2)}, u32[]{:S(2)}) collective-permute-start(bf16[256,1024]{1,0:T(8,128)(2,1)S(1)} %get-tuple-element.32), channel_id=1, source_target_pairs={{4,0},{8,4},{12,8},{16,12},{20,16},{24,20},{28,24},{32,28},{36,32}... | collective-permute-start | bytes 1572872 | tf_op jit(solution)/shard_map/ppermute | solution.py:16
  74.9 46.5 %collective-permute-start.9 = (bf16[256,1024]{1,0:T(8,128)(2,1)S(1)}, bf16[256,1024]{1,0:T(8,128)(2,1)S(1)}, u32[]{:S(2)}, u32[]{:S(2)}) collective-permute-start(bf16[256,1024]{1,0:T(8,128)(2,1)S(1)} %get-tuple-element.32), channel_id=1, source_target_pairs={{8,0},{12,4},{16,8},{20,12},{24,16},{28,20},{32,24},{36,28},{40,32... | collective-permute-start | bytes 1572872 | tf_op jit(solution)/shard_map/ppermute | solution.py:16
  77.9 46.8 %collective-permute-start.10 = (bf16[256,1024]{1,0:T(8,128)(2,1)S(1)}, bf16[256,1024]{1,0:T(8,128)(2,1)S(1)}, u32[]{:S(2)}, u32[]{:S(2)}) collective-permute-start(bf16[256,1024]{1,0:T(8,128)(2,1)S(1)} %get-tuple-element.32), channel_id=1, source_target_pairs={{12,0},{16,4},{20,8},{24,12},{28,16},{32,20},{36,24},{40,28},{44,3... | collective-permute-start | bytes 1572872 | tf_op jit(solution)/shard_map/ppermute | solution.py:16
  89.8 37.0 %collective-permute-start.11 = (bf16[256,1024]{1,0:T(8,128)(2,1)S(1)}, bf16[256,1024]{1,0:T(8,128)(2,1)S(1)}, u32[]{:S(2)}, u32[]{:S(2)}) collective-permute-start(bf16[256,1024]{1,0:T(8,128)(2,1)S(1)} %get-tuple-element.32), channel_id=1, source_target_pairs={{16,0},{20,4},{24,8},{28,12},{32,16},{36,20},{40,24},{44,28},{48,3... | collective-permute-start | bytes 1572872 | tf_op jit(solution)/shard_map/ppermute | solution.py:16
  91.8 35.8 %collective-permute-start.12 = (bf16[256,1024]{1,0:T(8,128)(2,1)S(1)}, bf16[256,1024]{1,0:T(8,128)(2,1)S(1)}, u32[]{:S(2)}, u32[]{:S(2)}) collective-permute-start(bf16[256,1024]{1,0:T(8,128)(2,1)S(1)} %get-tuple-element.32), channel_id=1, source_target_pairs={{20,0},{24,4},{28,8},{32,12},{36,16},{40,20},{44,24},{48,28},{52,3... | collective-permute-start | bytes 1572872 | tf_op jit(solution)/shard_map/ppermute | solution.py:16
  93.8 72.3 %copy-start = (bf16[256,1024]{1,0:T(8,128)(2,1)S(1)}, bf16[256,1024]{1,0:T(8,128)(2,1)}, u32[]{:S(2)}) copy-start(bf16[256,1024]{1,0:T(8,128)(2,1)} %v_ref.1) | copy-start | bytes 1572868
  93.8 72.3 %copy-start.1 = (bf16[256,1024]{1,0:T(8,128)(2,1)S(1)}, bf16[256,1024]{1,0:T(8,128)(2,1)}, u32[]{:S(2)}) copy-start(bf16[256,1024]{1,0:T(8,128)(2,1)} %k_ref.1) | copy-start | bytes 1572868
  93.8 72.3 %copy-start.2 = (bf16[256,1024]{1,0:T(8,128)(2,1)S(1)}, bf16[256,1024]{1,0:T(8,128)(2,1)}, u32[]{:S(2)}) copy-start(bf16[256,1024]{1,0:T(8,128)(2,1)} %q_ref.1) | copy-start | bytes 1572868
  93.8 72.3 %copy-start.3 = (bf16[256,1024]{1,0:T(8,128)(2,1)S(1)}, bf16[256,1024]{1,0:T(8,128)(2,1)}, u32[]{:S(2)}) copy-start(bf16[256,1024]{1,0:T(8,128)(2,1)} %ct_ref.1) | copy-start | bytes 1572868
  93.9 72.2 %copy-start.4 = (bf16[2304,1024]{1,0:T(8,128)(2,1)}, bf16[2304,1024]{1,0:T(8,128)(2,1)S(1)}, u32[]{:S(2)}) copy-start(bf16[2304,1024]{1,0:T(8,128)(2,1)S(1)} %constant_dynamic-update-slice_fusion.pext_ref) | copy-start | bytes 14155780
  93.9 50.9 %collective-permute-start.13 = (bf16[256,1024]{1,0:T(8,128)(2,1)S(1)}, bf16[256,1024]{1,0:T(8,128)(2,1)S(1)}, u32[]{:S(2)}, u32[]{:S(2)}) collective-permute-start(bf16[256,1024]{1,0:T(8,128)(2,1)S(1)} %get-tuple-element.32), channel_id=1, source_target_pairs={{24,0},{28,4},{32,8},{36,12},{40,16},{44,20},{48,24},{52,28},{56,3... | collective-permute-start | bytes 1572872 | tf_op jit(solution)/shard_map/ppermute | solution.py:16
  121.4 28.9 %collective-permute-start.14 = (bf16[256,1024]{1,0:T(8,128)(2,1)S(1)}, bf16[256,1024]{1,0:T(8,128)(2,1)S(1)}, u32[]{:S(2)}, u32[]{:S(2)}) collective-permute-start(bf16[256,1024]{1,0:T(8,128)(2,1)S(1)} %get-tuple-element.32), channel_id=1, source_target_pairs={{28,0},{32,4},{36,8},{40,12},{44,16},{48,20},{52,24},{56,28},{60,3... | collective-permute-start | bytes 1572872 | tf_op jit(solution)/shard_map/ppermute | solution.py:16
  124.7 40.6 %collective-permute-start.15 = (bf16[256,1024]{1,0:T(8,128)(2,1)S(1)}, bf16[256,1024]{1,0:T(8,128)(2,1)S(1)}, u32[]{:S(2)}, u32[]{:S(2)}) collective-permute-start(bf16[256,1024]{1,0:T(8,128)(2,1)S(1)} %get-tuple-element.32), channel_id=1, source_target_pairs={{32,0},{36,4},{40,8},{44,12},{48,16},{52,20},{56,24},{60,28},{64,3... | collective-permute-start | bytes 1572872 | tf_op jit(solution)/shard_map/ppermute | solution.py:16
  199.0 6.4 %collective-permute-start.16 = (f32[16,2048]{1,0:T(8,128)S(1)}, f32[16,2048]{1,0:T(8,128)S(1)}, u32[]{:S(2)}, u32[]{:S(2)}) collective-permute-start(f32[16,2048]{1,0:T(8,128)S(1)} %multiply_bitcast_fusion), channel_id=1, source_target_pairs={{0,1},{1,0},{2,3},{3,2},{4,5},{5,4},{6,7},{7,6},{8,9},{9,8},{10,11... | collective-permute-start | bytes 393224 | tf_op jit(solution)/shard_map/ppermute | solution.py:164
  205.4 6.6 %collective-permute-start.17 = (f32[16,2048]{1,0:T(8,128)S(1)}, f32[16,2048]{1,0:T(8,128)S(1)}, u32[]{:S(2)}, u32[]{:S(2)}) collective-permute-start(f32[16,2048]{1,0:T(8,128)S(1)} %fusion), channel_id=1, source_target_pairs={{0,2},{1,3},{2,0},{3,1},{4,6},{5,7},{6,4},{7,5},{8,10},{9,11},{10,... | collective-permute-start | bytes 393224 | tf_op jit(solution)/shard_map/ppermute | solution.py:164
  212.0 1.4 collective-permute-start.18
  213.4 5.6 %collective-permute-start.19 = (f32[16,2048]{1,0:T(8,128)S(1)}, f32[16,2048]{1,0:T(8,128)S(1)}, u32[]{:S(2)}, u32[]{:S(2)}) collective-permute-start(f32[16,2048]{1,0:T(8,128)S(1)} %add.53), channel_id=1, source_target_pairs={{0,8},{4,12},{8,0},{12,4},{16,24},{20,28},{24,16},{28,20},{32,40},... | collective-permute-start | bytes 393224 | tf_op jit(solution)/shard_map/ppermute | solution.py:164
  219.1 6.6 %collective-permute-start.20 = (f32[16,2048]{1,0:T(8,128)S(1)}, f32[16,2048]{1,0:T(8,128)S(1)}, u32[]{:S(2)}, u32[]{:S(2)}) collective-permute-start(f32[16,2048]{1,0:T(8,128)S(1)} %add.54), channel_id=1, source_target_pairs={{0,16},{4,20},{8,24},{12,28},{16,0},{20,4},{24,8},{28,12},{32,48},... | collective-permute-start | bytes 393224 | tf_op jit(solution)/shard_map/ppermute | solution.py:164
  225.6 6.1 %collective-permute-start.21 = (f32[16,2048]{1,0:T(8,128)S(1)}, f32[16,2048]{1,0:T(8,128)S(1)}, u32[]{:S(2)}, u32[]{:S(2)}) collective-permute-start(f32[16,2048]{1,0:T(8,128)S(1)} %add.55), channel_id=1, source_target_pairs={{0,32},{4,36},{8,40},{12,44},{16,48},{20,52},{24,56},{28,60},{32,0... | collective-permute-start | bytes 393224 | tf_op jit(solution)/shard_map/ppermute | solution.py:164
  231.7 6.6 %collective-permute-start.22 = (f32[16,2048]{1,0:T(8,128)S(1)}, f32[16,2048]{1,0:T(8,128)S(1)}, u32[]{:S(2)}, u32[]{:S(2)}) collective-permute-start(f32[16,2048]{1,0:T(8,128)S(1)} %add.56), channel_id=1, source_target_pairs={{0,64},{4,68},{8,72},{12,76},{16,80},{20,84},{24,88},{28,92},{32,9... | collective-permute-start | bytes 393224 | tf_op jit(solution)/shard_map/ppermute | solution.py:164
